TPU v7x, 128 devices: a whole 4x4x4 slice. The times are simulated.
128 devices in a mesh: row: 16 (over z_lo, x, core), col: 8 (over y, z_hi).
Axes of the slice: x: 4, y: 4, z: 4 (z_hi: 2, z_lo: 2; z = z_hi * 2 + z_lo), core: 2. Of those that a mesh axis runs over, the one named last changes fastest.
Arguments:
- shared_rows: float32 [2048, 16384], P('row', 'col'), may hold values from -0.125 to 0.125
- event_counts: int32 [16], replicated, may hold values from 32 to 128, as said below
- ridge: float32 [16384], P('col'), may hold values from 0.5 to 2
- items: float32 [1024, 16384], P('row', 'col'), may hold values from -6 to 6
- cand_ids: int32 [512], replicated, may hold values from 0 to 1023
- theta: float32 [16384], P('col'), may hold values from -0.046875 to 0.046875
Outputs:
- gram_tile: float32 [16384, 16384], P('row', 'col')
- scores: float32 [512], replicated
Inputs may be any that keep to these rules, and one draw needn't show every extreme that they name: event_counts[s] counts the live slots at the start of row shard s's 128 slots; some shard is full.
All inputs are finite; a program needn't handle non-finite values.
Results may differ from a plain program's by a relative error of at most 0.000068.
Values sent between devices are 32-bit elements; how exact they have to be, the bound alone decides.
No kernel may reach another device: no remote copies, remote signals or barrier semaphores. Data moves between devices by JAX's collectives and lax.ppermute only.
A program may use at most 128 MiB of HBM per device.

v0:
```python
import jax
import jax.numpy as jnp
from jax import lax
from jax.sharding import PartitionSpec as P

F = 16384
high = lax.Precision.HIGHEST


def spread(value, axis, source):
    kept = jnp.where(lax.axis_index(axis) == source, value, 0).astype(value.dtype)
    return lax.psum(kept, axis)


def body(shared_rows, event_counts, ridge, items, cand_ids, theta):
    ratio = lax.axis_size("row") // lax.axis_size("col")
    row_pos = lax.axis_index("row")
    col_pos = lax.axis_index("col")
    width_col = shared_rows.shape[1]
    width_row = width_col // ratio
    ev_slots = shared_rows.shape[0]
    slot = lax.iota(jnp.int32, ev_slots)
    masked = jnp.where((slot < event_counts[row_pos])[:, None], shared_rows, jnp.float32(0.0))
    offset = row_pos % ratio * width_row
    root = row_pos // ratio
    contract = (((0,), (0,)), ((), ()))
    col_all = lax.all_gather(masked, "row", axis=0, tiled=True)
    row_all = spread(lax.dynamic_slice_in_dim(col_all, offset, width_row, 1), "col", root)
    tile = lax.dot_general(
        row_all, col_all, contract, precision=high, preferred_element_type=jnp.float32
    )
    rows_global = row_pos * width_row + lax.broadcasted_iota(jnp.int32, (width_row, width_col), 0)
    cols_global = col_pos * width_col + lax.broadcasted_iota(jnp.int32, (width_row, width_col), 1)
    tile = tile + jnp.where(rows_global == cols_global, ridge[None, :], jnp.float32(0.0))
    items_dev = items.shape[0]
    onehot = (
        cand_ids[:, None] == row_pos * items_dev + lax.iota(jnp.int32, items_dev)[None, :]
    ).astype(jnp.float32)
    picked = jnp.dot(onehot, items, precision=high, preferred_element_type=jnp.float32)
    cand_col = lax.psum(picked, "row")
    across = (((1,), (1,)), ((), ()))
    cand_row = spread(lax.dynamic_slice_in_dim(cand_col, offset, width_row, 1), "col", root)
    image_part = lax.dot_general(
        cand_col, tile, across, precision=high, preferred_element_type=jnp.float32
    )
    image_row = lax.psum(image_part, "col")
    quad = jnp.where(col_pos == 0, jnp.sum(cand_row * image_row, axis=1), jnp.float32(0.0))
    linear = jnp.where(
        row_pos == 0,
        jnp.dot(cand_col, theta, precision=high, preferred_element_type=jnp.float32),
        jnp.float32(0.0),
    )
    quad_all, linear_all = lax.psum((quad, linear), ("row", "col"))
    return (tile, linear_all + jnp.sqrt(quad_all / F))


def solution(mesh):
    return jax.shard_map(
        body,
        mesh=mesh,
        in_specs=(P("row", "col"), P(), P("col"), P("row", "col"), P(), P("col")),
        out_specs=(P("row", "col"), P()),
        check_vma=False,
    )
```

profile of v0, /device:TPU:1, one launch (start us, length us, event | category | flops | bytes accessed | tf_op | source)
XLA Modules:
  0.0 940.3 jit_solution(5957106584917055528)
XLA Ops:
  7.2 0.0 copy-start
  7.2 0.0 all-gather.2.cloned.1.call-start
  7.2 1.3 dynamic_slice.9
  8.5 0.6 iota_compare_fusion
  9.2 2.3 broadcast_select_fusion
  11.5 0.0 all-gather.2.cloned.1.call-update
  11.5 0.0 all-reduce.8.cloned.1.call-start
  11.6 0.0 copy-done
  11.6 4.5 fusion
  16.1 0.0 all-reduce.8.cloned.1.call-update
  16.1 0.0 all-reduce.6.cloned.1.call-start
  16.2 90.8 %all-gather.2.cloned.1.call-done = f32[2048,2048]{1,0:T(8,128)} async-done(((f32[128,2048]{1,0:T(8,128)}), f32[2048,2048]{1,0:T(8,128)}) %all-gather.2.cloned.1.call-update) | async-done | bytes 16777232 | tf_op jit(solution)/shard_map/all_gather | solution.py:27
  107.0 8.7 dynamic-slice_select_fusion
  115.7 0.0 copy-start.3
  115.7 0.0 all-reduce.6.cloned.1.call-update
  115.7 0.0 all-reduce.10.cloned.1.call-start
  115.8 122.9 %all-reduce.8.cloned.1.call-done = f32[512,2048]{1,0:T(8,128)} async-done(((f32[512,2048]{1,0:T(8,128)}), f32[512,2048]{1,0:T(8,128)}) %all-reduce.8.cloned.1.call-update) | async-done | bytes 4194320 | tf_op jit(solution)/shard_map/psum | solution.py:40
  238.7 3.2 dynamic-slice_select_fusion.1
  241.9 343.4 %all-reduce.6.cloned.1.call-done = f32[2048,1024]{1,0:T(8,128)} async-done(((f32[2048,1024]{1,0:T(8,128)}), f32[2048,1024]{1,0:T(8,128)}) %all-reduce.6.cloned.1.call-update) | async-done | bytes 8388624 | tf_op jit(solution)/shard_map/psum | solution.py:12
  585.3 0.0 copy-done.3
  585.3 0.0 copy-start.1
  585.3 67.7 %select_add_fusion = f32[1024,2048]{1,0:T(8,128)S(1)} fusion(f32[2048]{0:T(1024)S(1)} %copy-done.3, s32[2048]{0:T(1024)S(1)} %iota_add_fusion, s32[1024]{0:T(1024)S(1)} %iota_add_fusion.1, f32[2048,1024]{1,0:T(8,128)} %all-reduce.6.cloned.1.call-done, f32[2048,2048]{1,0:T(8,128)} %all-gather.2.cloned.1.call-done), kind=kOutput, calls=%fused_computation | convolution fusion | flops 51545899008 | bytes 33574912 | tf_op jit(solution)/shard_map/dot_general | solution.py:29
  653.1 0.0 copy-start.4
  653.1 3.4 copy-done.4
  656.5 0.0 copy-done.1
  656.5 0.0 copy-start.2
  656.5 15.2 %fusion.5 = f32[512,1024]{1,0:T(8,128)} fusion(f32[512,2048]{1,0:T(8,128)S(1)} %copy-done.1, f32[1024,2048]{1,0:T(8,128)S(1)} %select_add_fusion), kind=kOutput, calls=%fused_computation.17 | convolution fusion | flops 12884901888 | bytes 14680064 | tf_op jit(solution)/shard_map/dot_general | solution.py:43
  671.7 0.0 all-reduce.10.cloned.1.call-update
  671.7 0.0 copy-done.2
  671.7 5.8 fusion.4
  677.5 185.2 %all-reduce.10.cloned.1.call-done = (f32[512,1024]{1,0:T(8,128)}, f32[512,1024]{1,0:T(8,128)}) async-done(((f32[512,1024]{1,0:T(8,128)}, f32[512,1024]{1,0:T(8,128)}), (f32[512,1024]{1,0:T(8,128)}, f32[512,1024]{1,0:T(8,128)})) %all-reduce.10.cloned.1.call-update) | async-done | bytes 4194320 | tf_op jit(solution)/shard_map/psum | solution.py:12
  862.7 2.5 multiply_reduce_fusion
  865.2 67.8 %all-reduce = (f32[512]{0:T(512)S(1)}, f32[512]{0:T(512)S(1)}) all-reduce(f32[512]{0:T(512)S(1)} %broadcast_select_fusion.2, f32[512]{0:T(512)S(1)} %broadcast_select_fusion.1), channel_id=1, replica_groups=mesh['row'=16,'col'=8] {'row','col'}, use_global_device_ids=true, to_apply=%region_2.3 | all-reduce | flops 1024 | bytes 8192 | tf_op jit(solution)/shard_map/psum | solution.py:53
  933.0 0.6 sqrt_add_fusion
  (5 shorter events, 0.0 us)
Async XLA Ops:
  7.2 4.4 copy-start
  7.2 99.8 %all-gather.2.cloned.1.call-start = ((), (), s32[]{:S(2)}) async-start(), calls=%async_computation | async-start | bytes 17825792 | tf_op jit(solution)/shard_map/all_gather | solution.py:27
  11.5 227.2 %all-reduce.8.cloned.1.call-start = ((), (), s32[]{:S(2)}) async-start(), calls=%async_computation.2 | async-start | bytes 8388608 | tf_op jit(solution)/shard_map/psum | solution.py:40
  16.1 569.2 %all-reduce.6.cloned.1.call-start = ((), (), s32[]{:S(2)}) async-start(), calls=%async_computation.1 | async-start | bytes 16777216 | tf_op jit(solution)/shard_map/psum | solution.py:12
  115.7 469.7 %copy-start.3 = (f32[2048]{0:T(1024)S(1)}, f32[2048]{0:T(1024)}, u32[]{:S(2)}) copy-start(f32[2048]{0:T(1024)} %param.8) | copy-start | bytes 24580
  115.7 747.0 %all-reduce.10.cloned.1.call-start = ((), (), s32[]{:S(2)}) async-start(), calls=%async_computation.3 | async-start | bytes 8388608 | tf_op jit(solution)/shard_map/psum | solution.py:12
  585.3 71.1 %copy-start.1 = (f32[512,2048]{1,0:T(8,128)S(1)}, f32[512,2048]{1,0:T(8,128)}, u32[]{:S(2)}) copy-start(f32[512,2048]{1,0:T(8,128)} %all-reduce.8.cloned.1.call-done) | copy-start | bytes 12582916
  653.1 3.4 copy-start.4
  656.5 15.3 %copy-start.2 = (f32[2048]{0:T(1024)S(1)}, f32[2048]{0:T(1024)}, u32[]{:S(2)}) copy-start(f32[2048]{0:T(1024)} %param.11) | copy-start | bytes 24580
Sparse Core Ops, SparseCore 0:
  11.7 95.2 all-gather.1
  109.5 129.1 all-reduce.7
  241.8 343.4 all-reduce.5
  671.8 190.8 all-reduce.9
where the time goes:
time: 944 us; the launch traced here: 940 us
  waiting for transfers between devices  742 us (79%)
  matrix products  93.2 us (10%)
  blocking collectives  67.8 us (7%)
  other arithmetic  18 us (2%)
  between operations  14.1 us (1%)
    psum x2, waiting for transfers between devices, spread(): return lax.psum(kept, axis)  529 us
    psum x1, waiting for transfers between devices, body(): cand_col = lax.psum(picked, 'row')  123 us
    all_gather x1, waiting for transfers between devices, body(): col_all = lax.all_gather(masked, 'row', axis=0, tiled=True)  90.8 us
    psum x1, blocking collectives, body(): quad_all, linear_all = lax.psum((quad, linear), ('row', 'col'))  67.8 us
    dot_general x1, matrix products, body(): lax.dot_general(row_all, col_all, contract, precision=high, preferred_ele...  67.7 us
  transfers between devices with their start and end apart: 4, of which 4 were waited for; matrix products, arithmetic and copies ran while one was open for 2% of the time, Pallas kernels for 0%

commit v1 on v0

--- a/solution.py
+++ b/solution.py
@@ -50,7 +50,7 @@
         jnp.dot(cand_col, theta, precision=high, preferred_element_type=jnp.float32),
         jnp.float32(0.0),
     )
-    quad_all, linear_all = lax.psum((quad, linear), ("row", "col"))
+    quad_all, linear_all = lax.psum(lax.psum((quad, linear), "row"), "col")
     return (tile, linear_all + jnp.sqrt(quad_all / F))
 
 

time: 944 us -> 916 us (0.970)
  blocking collectives: 67.8 us -> 46.7 us
    psum x1 -> x2, blocking collectives: 67.8 us -> 46.7 us  [body(): quad_all, linear_all = lax.psum(lax.psum((quad, linear), 'row'), 'col')]
where the time goes in v1:
time: 916 us; the launch traced here: 910 us
  waiting for transfers between devices  742 us (81%)
  matrix products  84.4 us (9%)
  blocking collectives  46.7 us (5%)
  other arithmetic  18 us (2%)
  between operations  13.9 us (2%)
    psum x2, waiting for transfers between devices, spread(): return lax.psum(kept, axis)  529 us
    psum x1, waiting for transfers between devices, body(): cand_col = lax.psum(picked, 'row')  123 us
    all_gather x1, waiting for transfers between devices, body(): col_all = lax.all_gather(masked, 'row', axis=0, tiled=True)  90.8 us
    dot_general x1, matrix products, body(): lax.dot_general(row_all, col_all, contract, precision=high, preferred_ele...  58.9 us
    psum x2, blocking collectives, body(): quad_all, linear_all = lax.psum(lax.psum((quad, linear), 'row'), 'col')  46.7 us
  transfers between devices with their start and end apart: 4, of which 4 were waited for; matrix products, arithmetic and copies ran while one was open for 2% of the time, Pallas kernels for 0%

profile of v1, /device:TPU:1, one launch (start us, length us, event | category | flops | bytes accessed | tf_op | source)
XLA Modules:
  0.0 910.2 jit_solution(13510939555130197497)
XLA Ops:
  7.2 0.0 copy-start
  7.2 0.0 all-gather.2.cloned.1.call-start
  7.2 1.3 dynamic_slice.9
  8.5 0.6 iota_compare_fusion
  9.2 2.3 broadcast_select_fusion
  11.5 0.0 all-gather.2.cloned.1.call-update
  11.5 0.0 all-reduce.9.cloned.1.call-start
  11.6 0.0 copy-done
  11.6 4.5 fusion
  16.1 0.0 all-reduce.9.cloned.1.call-update
  16.1 0.0 all-reduce.7.cloned.1.call-start
  16.2 90.8 %all-gather.2.cloned.1.call-done = f32[2048,2048]{1,0:T(8,128)} async-done(((f32[128,2048]{1,0:T(8,128)}), f32[2048,2048]{1,0:T(8,128)}) %all-gather.2.cloned.1.call-update) | async-done | bytes 16777232 | tf_op jit(solution)/shard_map/all_gather | solution.py:27
  107.0 8.7 dynamic-slice_select_fusion
  115.7 0.0 copy-start.3
  115.7 0.0 all-reduce.7.cloned.1.call-update
  115.7 0.0 all-reduce.11.cloned.1.call-start
  115.8 122.9 %all-reduce.9.cloned.1.call-done = f32[512,2048]{1,0:T(8,128)} async-done(((f32[512,2048]{1,0:T(8,128)}), f32[512,2048]{1,0:T(8,128)}) %all-reduce.9.cloned.1.call-update) | async-done | bytes 4194320 | tf_op jit(solution)/shard_map/psum | solution.py:40
  238.7 3.2 dynamic-slice_select_fusion.1
  241.9 343.4 %all-reduce.7.cloned.1.call-done = f32[2048,1024]{1,0:T(8,128)} async-done(((f32[2048,1024]{1,0:T(8,128)}), f32[2048,1024]{1,0:T(8,128)}) %all-reduce.7.cloned.1.call-update) | async-done | bytes 8388624 | tf_op jit(solution)/shard_map/psum | solution.py:12
  585.3 0.0 copy-done.3
  585.3 0.0 copy-start.1
  585.3 58.9 %select_add_fusion = f32[1024,2048]{1,0:T(8,128)S(1)} fusion(f32[2048]{0:T(1024)S(1)} %copy-done.3, s32[2048]{0:T(1024)S(1)} %iota_add_fusion, s32[1024]{0:T(1024)S(1)} %iota_add_fusion.1, f32[2048,1024]{1,0:T(8,128)} %all-reduce.7.cloned.1.call-done, f32[2048,2048]{1,0:T(8,128)} %all-gather.2.cloned.1.call-done), kind=kOutput, calls=%fused_computation | convolution fusion | flops 51545899008 | bytes 33574912 | tf_op jit(solution)/shard_map/dot_general | solution.py:29
  644.2 0.0 copy-start.4
  644.2 3.4 copy-done.4
  647.6 0.0 copy-done.1
  647.6 0.0 copy-start.2
  647.6 15.3 %fusion.5 = f32[512,1024]{1,0:T(8,128)} fusion(f32[512,2048]{1,0:T(8,128)S(1)} %copy-done.1, f32[1024,2048]{1,0:T(8,128)S(1)} %select_add_fusion), kind=kOutput, calls=%fused_computation.17 | convolution fusion | flops 12884901888 | bytes 14680064 | tf_op jit(solution)/shard_map/dot_general | solution.py:43
  662.9 0.0 all-reduce.11.cloned.1.call-update
  662.9 0.0 copy-done.2
  662.9 5.8 fusion.4
  668.7 185.1 %all-reduce.11.cloned.1.call-done = (f32[512,1024]{1,0:T(8,128)}, f32[512,1024]{1,0:T(8,128)}) async-done(((f32[512,1024]{1,0:T(8,128)}, f32[512,1024]{1,0:T(8,128)}), (f32[512,1024]{1,0:T(8,128)}, f32[512,1024]{1,0:T(8,128)})) %all-reduce.11.cloned.1.call-update) | async-done | bytes 4194320 | tf_op jit(solution)/shard_map/psum | solution.py:12
  853.8 2.5 multiply_reduce_fusion
  856.3 27.2 %all-reduce = (f32[512]{0:T(512)S(1)}, f32[512]{0:T(512)S(1)}) all-reduce(f32[512]{0:T(512)S(1)} %broadcast_select_fusion.2, f32[512]{0:T(512)S(1)} %broadcast_select_fusion.1), channel_id=1, replica_groups=mesh['row'=16,'col'=8] {'row'}, use_global_device_ids=true, to_apply=%region_2.3 | all-reduce | flops 1024 | bytes 8192 | tf_op jit(solution)/shard_map/psum | solution.py:53
  883.5 19.5 %all-reduce.1 = (f32[512]{0:T(512)S(1)}, f32[512]{0:T(512)S(1)}) all-reduce(f32[512]{0:T(512)S(1)} %get-tuple-element.2, f32[512]{0:T(512)S(1)} %get-tuple-element.3), channel_id=1, replica_groups=mesh['row'=16,'col'=8] {'col'}, use_global_device_ids=true, to_apply=%region_3.4 | all-reduce | flops 1024 | bytes 8192 | tf_op jit(solution)/shard_map/psum | solution.py:53
  903.0 0.6 sqrt_add_fusion
  (5 shorter events, 0.0 us)
Async XLA Ops:
  7.2 4.4 copy-start
  7.2 99.8 %all-gather.2.cloned.1.call-start = ((), (), s32[]{:S(2)}) async-start(), calls=%async_computation | async-start | bytes 17825792 | tf_op jit(solution)/shard_map/all_gather | solution.py:27
  11.5 227.2 %all-reduce.9.cloned.1.call-start = ((), (), s32[]{:S(2)}) async-start(), calls=%async_computation.2 | async-start | bytes 8388608 | tf_op jit(solution)/shard_map/psum | solution.py:40
  16.1 569.2 %all-reduce.7.cloned.1.call-start = ((), (), s32[]{:S(2)}) async-start(), calls=%async_computation.1 | async-start | bytes 16777216 | tf_op jit(solution)/shard_map/psum | solution.py:12
  115.7 469.7 %copy-start.3 = (f32[2048]{0:T(1024)S(1)}, f32[2048]{0:T(1024)}, u32[]{:S(2)}) copy-start(f32[2048]{0:T(1024)} %param.8) | copy-start | bytes 24580
  115.7 738.2 %all-reduce.11.cloned.1.call-start = ((), (), s32[]{:S(2)}) async-start(), calls=%async_computation.3 | async-start | bytes 8388608 | tf_op jit(solution)/shard_map/psum | solution.py:12
  585.3 62.3 %copy-start.1 = (f32[512,2048]{1,0:T(8,128)S(1)}, f32[512,2048]{1,0:T(8,128)}, u32[]{:S(2)}) copy-start(f32[512,2048]{1,0:T(8,128)} %all-reduce.9.cloned.1.call-done) | copy-start | bytes 12582916
  644.2 3.4 copy-start.4
  647.6 15.3 %copy-start.2 = (f32[2048]{0:T(1024)S(1)}, f32[2048]{0:T(1024)}, u32[]{:S(2)}) copy-start(f32[2048]{0:T(1024)} %param.11) | copy-start | bytes 24580
Sparse Core Ops, SparseCore 0:
  11.7 95.2 all-gather.1
  109.5 129.1 all-reduce.8
  241.8 343.4 all-reduce.6
  663.0 190.7 all-reduce.10
